TPU v7x, 128 devices: a whole 4x4x4 slice. The times are simulated.
128 devices in a mesh: ctx: 16 (over y_lo, z, core), head: 8 (over x, y_hi).
Axes of the slice: x: 4, y: 4 (y_hi: 2, y_lo: 2; y = y_hi * 2 + y_lo), z: 4, core: 2. Of those that a mesh axis runs over, the one named last changes fastest.
Arguments:
- hidden_in: bfloat16 [4096, 8192], P('ctx', 'head'), may hold values from -90 to 90
- query_rows: bfloat16 [4096, 8192], P('ctx', 'head'), may hold values from -5 to 5
- key_rows: bfloat16 [4096, 1024], P('ctx', 'head'), may hold values from -5 to 5
- value_rows: bfloat16 [4096, 1024], P('ctx', 'head'), may hold values from -6 to 6
- out_weight: bfloat16 [8192, 8192], P('head'), may hold values from -0.0625 to 0.0625
- grad_out: bfloat16 [4096, 8192], P('ctx', 'head'), may hold values from -6 to 6
- answer_mask: int32 [4096], P('ctx'), may hold values 0 or 1
Outputs:
- grad_query: bfloat16 [4096, 8192], P('ctx', 'head')
- grad_key: bfloat16 [4096, 1024], P('ctx', 'head')
- grad_value: bfloat16 [4096, 1024], P('ctx', 'head')
- fisher_q: float32 [16, 64], P('ctx', 'head')
- fisher_o: float32 [16, 64], P('ctx', 'head')
All inputs are finite; a program needn't handle non-finite values. No bound on the sum of `answer_mask` on one device may be relied on, other than what follows from the above.
Results may differ from a plain program's by a relative error of at most 0.019.
Values may be sent and summed in bfloat16 or wider, within the bound.
No kernel may reach another device: no remote copies, remote signals or barrier semaphores. Data moves between devices by JAX's collectives and lax.ppermute only.
A program may use at most 128 MiB of HBM per device.

v0:
```python
import math
import jax
import jax.numpy as jnp
from jax import lax
from jax.sharding import PartitionSpec as P

D = 8192
HEADS = 64
KVH = 8
HD = 128
NEGATIVE = -1e30
EPSILON = 1e-06


def block_scores(query_group, key_block, scaling, row_pos, col_pos):
    scores = (
        jnp.einsum("tgd,kd->tgk", query_group, key_block, preferred_element_type=jnp.float32)
        * scaling
    )
    return jnp.where(row_pos[:, None, None] >= col_pos[None, None, :], scores, NEGATIVE)


def head_squares(left_side, right_side, head_dim):
    product = lax.dot_general(
        left_side, right_side, (((0,), (0,)), ((), ())), preferred_element_type=jnp.float32
    )
    shaped = (product * product).reshape(
        product.shape[0], right_side.shape[1] // head_dim, head_dim
    )
    return jnp.sum(shaped, axis=(0, 2))


def body(hidden_in, query_rows, key_rows, value_rows, out_weight, grad_out, answer_mask):
    tok_dev = query_rows.shape[0]
    head_dim = HD
    group_size = HEADS // KVH
    local_groups = key_rows.shape[1] // head_dim
    scaling = head_dim ** (-0.5)
    own_index = lax.axis_index("ctx")
    first_row = own_index * tok_dev
    loss_weight = 0.25 + answer_mask.astype(jnp.float32)
    weighted = (grad_out.astype(jnp.float32) * loss_weight[:, None]).astype(jnp.bfloat16)
    keys_all, values_all = (
        lax.all_gather(key_rows, "ctx", axis=0, tiled=True),
        lax.all_gather(value_rows, "ctx", axis=0, tiled=True),
    )
    tokens = keys_all.shape[0]
    block_rows = math.gcd(512, tokens)

    def fetch(table, block_number):
        return lax.dynamic_slice_in_dim(table, block_number * block_rows, block_rows, 0)

    def column_pos(block_number):
        return block_number * block_rows + jnp.arange(block_rows, dtype=jnp.int32)

    buffer = jnp.zeros((tokens, 2 * local_groups * head_dim), jnp.float32)
    rows = query_rows.shape[0]
    row_pos = first_row + jnp.arange(rows, dtype=jnp.int32)
    needed = (first_row + rows - 1) // block_rows + 1
    query_heads = query_rows.reshape(rows, local_groups, group_size, head_dim)
    log_totals = []
    shared_head = 0
    query_group = query_heads[:, shared_head]

    def stats_step(block_number, carried):
        running_max, running_sum = carried
        key_block = fetch(keys_all, block_number)
        scores = block_scores(query_group, key_block, scaling, row_pos, column_pos(block_number))
        new_max = jnp.maximum(running_max, jnp.max(scores, axis=-1))
        running_sum = running_sum * jnp.exp(running_max - new_max) + jnp.sum(
            jnp.exp(scores - new_max[..., None]), axis=-1
        )
        return (new_max, running_sum)

    start_max = jnp.full((rows, group_size), NEGATIVE, jnp.float32)
    start_sum = jnp.zeros((rows, group_size), jnp.float32)
    running_max, running_sum = lax.fori_loop(0, needed, stats_step, (start_max, start_sum))
    log_total = running_max + jnp.log(running_sum)

    def value_step(block_number, accumulated):
        key_block = fetch(keys_all, block_number)
        value_block = fetch(values_all, block_number)
        scores = block_scores(query_group, key_block, scaling, row_pos, column_pos(block_number))
        rounded = jnp.exp(scores - log_total[..., None]).astype(jnp.bfloat16)
        return accumulated + jnp.einsum(
            "tgk,kd->tgd", rounded, value_block, preferred_element_type=jnp.float32
        )

    accumulated = lax.fori_loop(
        0, needed, value_step, jnp.zeros((rows, group_size, head_dim), jnp.float32)
    )
    log_totals.append(log_total)
    attended_list = [accumulated.astype(jnp.bfloat16)]
    attended_part = jnp.stack(attended_list, axis=1).reshape(
        rows, local_groups * group_size * head_dim
    )
    log_totals, attended = (log_totals, attended_part)
    piece_part = lax.all_gather(weighted, "head", axis=1, tiled=True)
    grad_sum = lax.dot_general(
        piece_part, out_weight, (((1,), (1,)), ((), ())), preferred_element_type=jnp.float32
    )
    grad_sum, squares_out = (grad_sum, head_squares(piece_part, attended, head_dim))
    grad_attended, squares_out = (grad_sum.astype(jnp.bfloat16), squares_out)
    backward_buffer = buffer
    rows = query_rows.shape[0]
    backward_row_pos = first_row + jnp.arange(rows, dtype=jnp.int32)
    needed = (first_row + rows - 1) // block_rows + 1
    query_heads = query_rows.reshape(rows, local_groups, group_size, head_dim)
    grad_heads = grad_attended.reshape(rows, local_groups, group_size, head_dim)
    attended_heads = attended.reshape(rows, local_groups, group_size, head_dim)
    shared_head = 0
    backward_query_group = query_heads[:, shared_head]
    grad_group = grad_heads[:, shared_head]
    backward_log_total = log_totals[shared_head]
    row_dot = jnp.sum(
        grad_group.astype(jnp.float32) * attended_heads[:, shared_head].astype(jnp.float32), axis=-1
    )
    key_column = jnp.int32(shared_head * head_dim)
    value_column = jnp.int32((local_groups + shared_head) * head_dim)

    def back_step(block_number, carried):
        query_sum, buffer_now = carried
        key_block = fetch(keys_all, block_number)
        value_block = fetch(values_all, block_number)
        scores = block_scores(
            backward_query_group, key_block, scaling, backward_row_pos, column_pos(block_number)
        )
        softmax = jnp.exp(scores - backward_log_total[..., None])
        rounded = softmax.astype(jnp.bfloat16)
        grad_prob = jnp.einsum(
            "tgd,kd->tgk", grad_group, value_block, preferred_element_type=jnp.float32
        )
        grad_score = (softmax * (grad_prob - row_dot[..., None]) * scaling).astype(jnp.bfloat16)
        query_sum = query_sum + jnp.einsum(
            "tgk,kd->tgd", grad_score, key_block, preferred_element_type=jnp.float32
        )
        key_part = jnp.einsum(
            "tgk,tgd->kd", grad_score, backward_query_group, preferred_element_type=jnp.float32
        )
        value_part = jnp.einsum(
            "tgk,tgd->kd", rounded, grad_group, preferred_element_type=jnp.float32
        )
        row_start = (block_number * block_rows).astype(jnp.int32)
        old_key = lax.dynamic_slice(buffer_now, (row_start, key_column), (block_rows, head_dim))
        buffer_now = lax.dynamic_update_slice(
            buffer_now, old_key + key_part, (row_start, key_column)
        )
        old_value = lax.dynamic_slice(buffer_now, (row_start, value_column), (block_rows, head_dim))
        buffer_now = lax.dynamic_update_slice(
            buffer_now, old_value + value_part, (row_start, value_column)
        )
        return (query_sum, buffer_now)

    start_query = jnp.zeros((rows, group_size, head_dim), jnp.float32)
    query_sum, backward_buffer = lax.fori_loop(0, needed, back_step, (start_query, backward_buffer))
    query_grads = [query_sum.astype(jnp.bfloat16)]
    grad_query_part = jnp.stack(query_grads, axis=1).reshape(
        rows, local_groups * group_size * head_dim
    )
    key_sums = lax.psum_scatter(
        backward_buffer.astype(jnp.bfloat16), "ctx", scatter_dimension=0, tiled=True
    ).astype(jnp.float32)
    grad_key = key_sums[:, : local_groups * head_dim].astype(jnp.bfloat16)
    grad_value = key_sums[:, local_groups * head_dim :].astype(jnp.bfloat16)
    squares_query = head_squares(
        lax.all_gather(hidden_in, "head", axis=1, tiled=True), grad_query_part, head_dim
    )
    normal_size = D * head_dim * tok_dev
    fisher_q = jnp.log(squares_query / normal_size + EPSILON).reshape(1, -1)
    fisher_o = jnp.log(squares_out / normal_size + EPSILON).reshape(1, -1)
    return (grad_query_part, grad_key, grad_value, fisher_q, fisher_o)


def solution(mesh):
    return jax.shard_map(
        body,
        mesh=mesh,
        in_specs=(
            P("ctx", "head"),
            P("ctx", "head"),
            P("ctx", "head"),
            P("ctx", "head"),
            P("head", None),
            P("ctx", "head"),
            P("ctx"),
        ),
        out_specs=(
            P("ctx", "head"),
            P("ctx", "head"),
            P("ctx", "head"),
            P("ctx", "head"),
            P("ctx", "head"),
        ),
        check_vma=False,
    )
```

profile of v0, /device:TPU:0, one launch (start us, length us, event | category | flops | bytes accessed | tf_op | source)
XLA Modules:
  0.0 331.3 jit_solution(14228058823165366588)
XLA Ops:
  7.2 0.0 all-gather.5.cloned.1.call-start
  7.2 0.7 all-gather.5.cloned.1.call-update
  7.9 0.0 all-gather.7.cloned.1.call-start
  7.9 0.7 all-gather.7.cloned.1.call-update
  8.7 0.0 all-gather.9.cloned.1.call-start
  8.7 0.7 convert_add_fusion
  9.4 2.0 multiply_convert_fusion
  11.4 0.0 all-gather.9.cloned.1.call-update
  11.4 0.0 all-gather.11.cloned.1.call-start
  11.4 0.5 all-gather.11.cloned.1.call-update
  12.0 0.0 reduce-scatter.2.cloned.1.call-start
  12.0 1.2 copy.28
  13.3 0.3 copy.33
  13.6 31.2 %all-gather.5.cloned.1.call-done = bf16[4096,128]{1,0:T(8,128)(2,1)} async-done(((bf16[256,128]{1,0:T(8,128)(2,1)}), bf16[4096,128]{1,0:T(8,128)(2,1)}) %all-gather.5.cloned.1.call-update) | async-done | bytes 1048592 | tf_op jit(solution)/shard_map/all_gather | solution.py:44
  44.8 2.8 while.37
  44.8 0.1 broadcast_compare_fusion.6
  44.9 1.7 fusion.94
  46.7 0.9 exponential_reduce_fusion.2
  47.6 31.5 %all-gather.7.cloned.1.call-done = bf16[4096,128]{1,0:T(8,128)(2,1)} async-done(((bf16[256,128]{1,0:T(8,128)(2,1)}), bf16[4096,128]{1,0:T(8,128)(2,1)}) %all-gather.7.cloned.1.call-update) | async-done | bytes 1048592 | tf_op jit(solution)/shard_map/all_gather | solution.py:45
  79.0 0.1 broadcast.135.clone
  79.1 2.9 while.38
  79.2 0.1 broadcast_compare_fusion.7
  79.3 2.7 fusion.98
  82.0 0.2 copy.32
  82.3 71.2 %all-gather.9.cloned.1.call-done = bf16[256,8192]{1,0:T(8,128)(2,1)} async-done(((bf16[256,1024]{1,0:T(8,128)(2,1)}), bf16[256,8192]{1,0:T(8,128)(2,1)}) %all-gather.9.cloned.1.call-update) | async-done | bytes 4194320 | tf_op jit(solution)/shard_map/all_gather | solution.py:98
  153.4 11.6 %convolution_convert_fusion = bf16[256,1024]{1,0:T(8,128)(2,1)S(1)} fusion(bf16[256,8192]{1,0:T(8,128)(2,1)} %all-gather.9.cloned.1.call-done, bf16[1024,8192]{1,0:T(8,128)(2,1)} %param.17), kind=kOutput, calls=%fused_computation.63 | convolution fusion | flops 4295229440 | bytes 21495808 | tf_op jit(solution)/shard_map/dot_general | solution.py:99
  165.0 0.1 copy_bitcast_fusion.1
  165.1 0.1 copy.40
  165.2 0.3 copy.30
  165.5 0.2 multiply_reduce_fusion.2
  165.7 0.1 broadcast.135
  165.8 2.2 broadcast_in_dim.48
  168.0 11.3 %while.39 = (s32[]{:T(128)}, f32[256,8,128]{2,0,1:T(8,128)S(1)}, f32[4096,256]{1,0:T(8,128)}, s32[]{:T(128)}, bf16[4096,128]{1,0:T(8,128)(2,1)}, /*index=5*/bf16...) while((s32[]{:T(128)}, f32[256,8,128]{2,0,1:T(8,128)S(1)}, ...), condition=%wide.region_8.9_spmd.clone, body=%wide.region_7.8_spmd.clone.sunk | while | flops 1354236672 | bytes 24934616 | solution.py:155
  168.0 0.1 broadcast_compare_fusion.8
  168.2 1.6 fusion.109
  169.8 2.4 fusion.110
  172.2 1.8 convolution_add_fusion.2
  174.1 2.4 fusion.111
  176.5 2.8 fusion.112
  179.3 3.8 %convert_element_type.47 = bf16[4096,256]{1,0:T(8,128)(2,1)} convert(f32[4096,256]{1,0:T(8,128)} %get-tuple-element.150) | non-fusion elementwise | flops 1048576 | bytes 6291456 | tf_op jit(solution)/shard_map/convert_element_type | solution.py:161
  183.0 0.0 reduce-scatter.2.cloned.1.call-update
  183.1 7.0 %multiply_reduce_fusion = f32[1024]{0:T(1024)S(1)} fusion(bf16[256,8192]{1,0:T(8,128)(2,1)} %all-gather.9.cloned.1.call-done, bf16[256,1024]{0,1:T(8,128)(2,1)S(1)} %bitcast.153), kind=kOutput, calls=%fused_computation.61 | convolution fusion | flops 4311743488 | bytes 4722688 | tf_op jit(solution)/shard_map/dot_general | solution.py:24
  190.1 0.1 bitcast_reduce_fusion
  190.2 0.1 copy_bitcast_fusion
  190.3 0.0 copy-start
  190.3 34.7 %all-gather.11.cloned.1.call-done = bf16[256,8192]{1,0:T(8,128)(2,1)} async-done(((bf16[256,1024]{1,0:T(8,128)(2,1)}), bf16[256,8192]{1,0:T(8,128)(2,1)}) %all-gather.11.cloned.1.call-update) | async-done | bytes 4194320 | tf_op jit(solution)/shard_map/all_gather | solution.py:166
  225.1 7.1 %multiply_reduce_fusion.1 = f32[1024]{0:T(1024)S(1)} fusion(bf16[256,1024]{1,0:T(8,128)(2,1)S(1)} %copy_bitcast_fusion, bf16[256,8192]{1,0:T(8,128)(2,1)} %all-gather.11.cloned.1.call-done), kind=kOutput, calls=%fused_computation.62 | convolution fusion | flops 4311743488 | bytes 4722688 | tf_op jit(solution)/shard_map/dot_general | solution.py:24
  232.2 0.0 copy-done
  232.2 0.1 bitcast_reduce_fusion.1
  232.3 0.5 log_bitcast_fusion
  232.8 0.5 log_bitcast_fusion.1
  233.4 89.9 %reduce-scatter.2.cloned.1.call-done = bf16[256,256]{1,0:T(8,128)(2,1)} async-done(((bf16[4096,256]{1,0:T(8,128)(2,1)}), bf16[256,256]{1,0:T(8,128)(2,1)}) %reduce-scatter.2.cloned.1.call-update) | async-done | bytes 131088 | tf_op jit(solution)/shard_map/reduce_scatter | solution.py:160
  323.3 1.5 fusion.57
  (12 shorter events, 0.0 us)
Async XLA Ops:
  7.2 37.6 %all-gather.5.cloned.1.call-start = ((), (), s32[]{:S(2)}) async-start(), calls=%async_computation.1 | async-start | bytes 1114112 | tf_op jit(solution)/shard_map/all_gather | solution.py:44
  7.9 71.1 %all-gather.7.cloned.1.call-start = ((), (), s32[]{:S(2)}) async-start(), calls=%async_computation.2 | async-start | bytes 1114112 | tf_op jit(solution)/shard_map/all_gather | solution.py:45
  8.7 144.8 %all-gather.9.cloned.1.call-start = ((), (), s32[]{:S(2)}) async-start(), calls=%async_computation.3 | async-start | bytes 4718592 | tf_op jit(solution)/shard_map/all_gather | solution.py:98
  11.4 213.7 %all-gather.11.cloned.1.call-start = ((), (), s32[]{:S(2)}) async-start(), calls=%async_computation.5 | async-start | bytes 4718592 | tf_op jit(solution)/shard_map/all_gather | solution.py:166
  12.0 311.3 %reduce-scatter.2.cloned.1.call-start = ((), (), s32[]{:S(2)}) async-start(), calls=%async_computation.4 | async-start | bytes 2228224 | tf_op jit(solution)/shard_map/reduce_scatter | solution.py:160
  190.3 41.9 %copy-start = (bf16[256,1024]{1,0:T(8,128)(2,1)}, bf16[256,1024]{1,0:T(8,128)(2,1)S(1)}, u32[]{:S(2)}) copy-start(bf16[256,1024]{1,0:T(8,128)(2,1)S(1)} %copy_bitcast_fusion) | copy-start | bytes 1572868
Sparse Core Ops, SparseCore 0:
  9.7 35.0 all-gather.4
  46.5 32.5 all-gather.6
  82.0 71.3 all-gather.8
  155.6 69.3 all-gather.10
  227.3 95.9 reduce-scatter.1
where the time goes:
time: 333 us; the launch traced here: 331 us
  waiting for transfers between devices  260 us (78%)
  matrix products  41.2 us (12%)
  between operations  13.9 us (4%)
  other arithmetic  9.25 us (3%)
  local copies, waits for them, and re-layouts  6.17 us (2%)
    reduce_scatter x1, waiting for transfers between devices, body(): lax.psum_scatter(backward_buffer.astype(jnp.bfloat16), 'ctx', scatter_dim...  89.9 us
    all_gather x1, waiting for transfers between devices, body(): piece_part = lax.all_gather(weighted, 'head', axis=1, tiled=True)  71.2 us
    all_gather x1, waiting for transfers between devices, body(): lax.all_gather(hidden_in, 'head', axis=1, tiled=True)  34.7 us
    all_gather x1, waiting for transfers between devices, body(): lax.all_gather(value_rows, 'ctx', axis=0, tiled=True)  31.5 us
    all_gather x1, waiting for transfers between devices, body(): lax.all_gather(key_rows, 'ctx', axis=0, tiled=True)  31.2 us
    dot_general x2, matrix products, head_squares(): lax.dot_general(left_side, right_side, (((0,), (0,)), ((), ())), preferre...  14.2 us
    dot_general x1, matrix products, body(): lax.dot_general(piece_part, out_weight, (((1,), (1,)), ((), ())), preferr...  11.6 us
  transfers between devices with their start and end apart: 5, of which 5 were waited for; matrix products, arithmetic and copies ran while one was open for 17% of the time, Pallas kernels for 0%

commit v1 on v0

--- a/solution.py
+++ b/solution.py
@@ -95,7 +95,8 @@
         rows, local_groups * group_size * head_dim
     )
     log_totals, attended = (log_totals, attended_part)
-    piece_part = lax.all_gather(weighted, "head", axis=1, tiled=True)
+    stack = jnp.stack([weighted] * lax.axis_size("head"))
+    piece_part = jnp.concatenate(lax.all_to_all(stack, "head", 0, 0), axis=1)
     grad_sum = lax.dot_general(
         piece_part, out_weight, (((1,), (1,)), ((), ())), preferred_element_type=jnp.float32
     )

time: 333 us -> 317 us (0.952)
  waiting for transfers between devices: 260 us -> 236 us
  starting transfers between devices: 0.19 us -> 7.3 us
    all_gather x1 -> x0, waiting for transfers between devices: 71.2 us -> none  [body(): piece_part = lax.all_gather(weighted, 'head', axis=1, tiled=True)]
    reduce_scatter x1, waiting for transfers between devices: 89.9 us -> 113 us  [body(): lax.psum_scatter(backward_buffer.astype(jnp.bfloat16), 'ctx', scatter_dim...]
    all_gather x1, waiting for transfers between devices: 31.2 us -> 53.8 us  [body(): lax.all_gather(key_rows, 'ctx', axis=0, tiled=True)]
    all_to_all x0 -> x1, starting transfers between devices: none -> 7.15 us  [body(): piece_part = jnp.concatenate(lax.all_to_all(stack, 'head', 0, 0), axis=1)]
  transfers between devices with their start and end apart: 5 -> 5, of which waited for: 5 -> 4; matrix products, arithmetic and copies ran while one was open for 17% -> 18% of each run, Pallas kernels for 0% -> 0%
where the time goes in v1:
time: 317 us; the launch traced here: 315 us
  waiting for transfers between devices  236 us (74%)
  matrix products  41.3 us (13%)
  between operations  13.9 us (4%)
  other arithmetic  8.46 us (3%)
  local copies, waits for them, and re-layouts  7.58 us (2%)
  starting transfers between devices  7.3 us (2%)
    reduce_scatter x1, waiting for transfers between devices, body(): lax.psum_scatter(backward_buffer.astype(jnp.bfloat16), 'ctx', scatter_dim...  113 us
    all_gather x1, waiting for transfers between devices, body(): lax.all_gather(key_rows, 'ctx', axis=0, tiled=True)  53.8 us
    all_gather x1, waiting for transfers between devices, body(): lax.all_gather(value_rows, 'ctx', axis=0, tiled=True)  34 us
    all_gather x1, waiting for transfers between devices, body(): lax.all_gather(hidden_in, 'head', axis=1, tiled=True)  33.1 us
    dot_general x2, matrix products, head_squares(): lax.dot_general(left_side, right_side, (((0,), (0,)), ((), ())), preferre...  14.1 us
    dot_general x1, matrix products, body(): lax.dot_general(piece_part, out_weight, (((1,), (1,)), ((), ())), preferr...  11.6 us
    all_to_all x1, starting transfers between devices, body(): piece_part = jnp.concatenate(lax.all_to_all(stack, 'head', 0, 0), axis=1)  7.15 us
  transfers between devices with their start and end apart: 5, of which 4 were waited for; matrix products, arithmetic and copies ran while one was open for 18% of the time, Pallas kernels for 0%

profile of v1, /device:TPU:0, one launch (start us, length us, event | category | flops | bytes accessed | tf_op | source)
XLA Modules:
  0.0 315.0 jit_solution(2720503980437639266)
XLA Ops:
  7.2 0.0 all-gather.4.cloned.1.call-start
  7.2 0.7 all-gather.4.cloned.1.call-update
  7.9 0.0 all-gather.6.cloned.1.call-start
  7.9 0.7 all-gather.6.cloned.1.call-update
  8.6 0.7 convert_add_fusion
  9.3 1.2 multiply_convert_fusion
  10.5 0.2 copy.31
  10.7 2.2 stack.2
  13.0 0.0 copy-start.1
  13.0 7.1 %all-to-all-start = ((bf16[8,256,1024]{1,2,0:T(8,128)(2,1)}), bf16[8,256,1024]{1,2,0:T(8,128)(2,1)}, u32[]{:S(2)}, u32[]{:S(2)}) async-start(bf16[8,256,1024]{1,2,0:T(8,128)(2,1)} %stack.2), calls=%async_computation | async-start | bytes 8388608 | tf_op jit(solution)/shard_map/all_to_all | solution.py:99
  20.1 0.0 all-gather.8.cloned.1.call-start
  20.2 0.7 all-gather.8.cloned.1.call-update
  20.9 0.0 reduce-scatter.2.cloned.1.call-start
  20.9 0.0 copy-done.1
  20.9 0.2 copy.29
  21.1 0.3 copy.35
  21.4 53.8 %all-gather.4.cloned.1.call-done = bf16[4096,128]{1,0:T(8,128)(2,1)} async-done(((bf16[256,128]{1,0:T(8,128)(2,1)}), bf16[4096,128]{1,0:T(8,128)(2,1)}) %all-gather.4.cloned.1.call-update) | async-done | bytes 1048592 | tf_op jit(solution)/shard_map/all_gather | solution.py:44
  75.3 2.8 while.37
  75.3 0.1 broadcast_compare_fusion.6
  75.4 1.7 fusion.94
  77.1 0.9 exponential_reduce_fusion.2
  78.1 34.0 %all-gather.6.cloned.1.call-done = bf16[4096,128]{1,0:T(8,128)(2,1)} async-done(((bf16[256,128]{1,0:T(8,128)(2,1)}), bf16[4096,128]{1,0:T(8,128)(2,1)}) %all-gather.6.cloned.1.call-update) | async-done | bytes 1048592 | tf_op jit(solution)/shard_map/all_gather | solution.py:45
  112.0 0.1 broadcast.137.clone
  112.1 2.9 while.38
  112.2 0.1 broadcast_compare_fusion.7
  112.3 2.7 fusion.98
  115.0 0.2 copy.34
  115.3 0.0 all-to-all-done
  115.3 11.6 %convolution_convert_fusion = bf16[256,1024]{1,0:T(8,128)(2,1)S(1)} fusion(bf16[256,8192]{0,1:T(8,128)(2,1)} %bitcast.2, bf16[1024,8192]{1,0:T(8,128)(2,1)} %param.17), kind=kOutput, calls=%fused_computation.63 | convolution fusion | flops 4295229440 | bytes 21495808 | tf_op jit(solution)/shard_map/dot_general | solution.py:100
  126.9 0.1 copy_bitcast_fusion.1
  127.0 0.1 copy.42
  127.1 0.3 copy.32
  127.4 0.2 multiply_reduce_fusion.2
  127.6 0.1 broadcast.137
  127.7 2.2 broadcast_in_dim.48
  129.9 11.3 %while.39 = (s32[]{:T(128)}, f32[256,8,128]{2,0,1:T(8,128)S(1)}, f32[4096,256]{1,0:T(8,128)}, s32[]{:T(128)}, bf16[4096,128]{1,0:T(8,128)(2,1)}, /*index=5*/bf16...) while((s32[]{:T(128)}, f32[256,8,128]{2,0,1:T(8,128)S(1)}, ...), condition=%wide.region_8.9_spmd.clone, body=%wide.region_7.8_spmd.clone.sunk | while | flops 1354236672 | bytes 24934616 | solution.py:156
  129.9 0.1 broadcast_compare_fusion.8
  130.1 1.6 fusion.109
  131.7 2.4 fusion.110
  134.1 1.8 convolution_add_fusion.2
  136.0 2.4 fusion.111
  138.4 2.8 fusion.112
  141.2 3.8 %convert_element_type.47 = bf16[4096,256]{1,0:T(8,128)(2,1)} convert(f32[4096,256]{1,0:T(8,128)} %get-tuple-element.150) | non-fusion elementwise | flops 1048576 | bytes 6291456 | tf_op jit(solution)/shard_map/convert_element_type | solution.py:162
  145.0 0.0 reduce-scatter.2.cloned.1.call-update
  145.0 7.0 %multiply_reduce_fusion = f32[1024]{0:T(1024)S(1)} fusion(bf16[256,8192]{0,1:T(8,128)(2,1)} %bitcast.2, bf16[256,1024]{0,1:T(8,128)(2,1)S(1)} %bitcast.156), kind=kOutput, calls=%fused_computation.61 | convolution fusion | flops 4311743488 | bytes 4722688 | tf_op jit(solution)/shard_map/dot_general | solution.py:24
  152.0 0.1 bitcast_reduce_fusion
  152.1 0.5 log_bitcast_fusion
  152.6 0.1 copy_bitcast_fusion
  152.7 0.0 copy-start
  152.7 33.1 %all-gather.8.cloned.1.call-done = bf16[256,8192]{1,0:T(8,128)(2,1)} async-done(((bf16[256,1024]{1,0:T(8,128)(2,1)}), bf16[256,8192]{1,0:T(8,128)(2,1)}) %all-gather.8.cloned.1.call-update) | async-done | bytes 4194320 | tf_op jit(solution)/shard_map/all_gather | solution.py:167
  185.8 7.1 %multiply_reduce_fusion.1 = f32[1024]{0:T(1024)S(1)} fusion(bf16[256,1024]{1,0:T(8,128)(2,1)S(1)} %copy_bitcast_fusion, bf16[256,8192]{1,0:T(8,128)(2,1)} %all-gather.8.cloned.1.call-done), kind=kOutput, calls=%fused_computation.62 | convolution fusion | flops 4311743488 | bytes 4722688 | tf_op jit(solution)/shard_map/dot_general | solution.py:24
  193.0 0.0 copy-done
  193.0 0.1 bitcast_reduce_fusion.1
  193.1 0.5 log_bitcast_fusion.1
  193.6 113.3 %reduce-scatter.2.cloned.1.call-done = bf16[256,256]{1,0:T(8,128)(2,1)} async-done(((bf16[4096,256]{1,0:T(8,128)(2,1)}), bf16[256,256]{1,0:T(8,128)(2,1)}) %reduce-scatter.2.cloned.1.call-update) | async-done | bytes 131088 | tf_op jit(solution)/shard_map/reduce_scatter | solution.py:161
  307.0 1.5 fusion.57
  (12 shorter events, 0.0 us)
Async XLA Ops:
  7.2 68.1 %all-gather.4.cloned.1.call-start = ((), (), s32[]{:S(2)}) async-start(), calls=%async_computation.2 | async-start | bytes 1114112 | tf_op jit(solution)/shard_map/all_gather | solution.py:44
  7.9 104.1 %all-gather.6.cloned.1.call-start = ((), (), s32[]{:S(2)}) async-start(), calls=%async_computation.3 | async-start | bytes 1114112 | tf_op jit(solution)/shard_map/all_gather | solution.py:45
  13.0 7.9 %copy-start.1 = (bf16[256,1024]{1,0:T(8,128)(2,1)S(1)}, bf16[256,1024]{1,0:T(8,128)(2,1)}, u32[]{:S(2)}) copy-start(bf16[256,1024]{1,0:T(8,128)(2,1)} %param.14) | copy-start | bytes 1572868
  13.0 102.3 %all-to-all-start = ((bf16[8,256,1024]{1,2,0:T(8,128)(2,1)}), bf16[8,256,1024]{1,2,0:T(8,128)(2,1)}, u32[]{:S(2)}, u32[]{:S(2)}) async-start(bf16[8,256,1024]{1,2,0:T(8,128)(2,1)} %stack.2), calls=%async_computation | async-start | bytes 8388608 | tf_op jit(solution)/shard_map/all_to_all | solution.py:99
  20.1 165.7 %all-gather.8.cloned.1.call-start = ((), (), s32[]{:S(2)}) async-start(), calls=%async_computation.5 | async-start | bytes 4718592 | tf_op jit(solution)/shard_map/all_gather | solution.py:167
  20.9 286.1 %reduce-scatter.2.cloned.1.call-start = ((), (), s32[]{:S(2)}) async-start(), calls=%async_computation.4 | async-start | bytes 2228224 | tf_op jit(solution)/shard_map/reduce_scatter | solution.py:161
  152.7 40.3 %copy-start = (bf16[256,1024]{1,0:T(8,128)(2,1)}, bf16[256,1024]{1,0:T(8,128)(2,1)S(1)}, u32[]{:S(2)}) copy-start(bf16[256,1024]{1,0:T(8,128)(2,1)S(1)} %copy_bitcast_fusion) | copy-start | bytes 1572868
Sparse Core Ops, SparseCore 0:
  9.7 65.5 all-gather.3
  77.0 35.0 all-gather.5
  114.4 71.3 all-gather.7
  188.1 118.8 reduce-scatter.1
